TPU v7x, 32 devices: a whole 2x2x4 slice. The times are simulated.
32 devices in a mesh: band: 16 (over z, x, core), chan: 2 (over y).
Axes of the slice: x: 2, y: 2, z: 4, core: 2. Of those that a mesh axis runs over, the one named last changes fastest.
Arguments:
- features: bfloat16 [256, 64, 1024], P('chan', 'band'), may hold values from -6 to 6
- depth_kernel: bfloat16 [3, 9, 256], P(None, None, 'chan'), may hold values from -2 to 2
- pointwise: bfloat16 [4, 256, 256], P(None, 'chan'), may hold values from -0.25 to 0.25
- cotangent: bfloat16 [256, 64, 1024], P('chan', 'band'), may hold values from -6 to 6
Outputs:
- output: bfloat16 [256, 64, 1024], P('chan', 'band')
- grad_input: float32 [256, 64, 1024], P('chan', 'band')
- grad_depth: float32 [3, 9, 256], P(None, None, 'chan')
- grad_point: float32 [4, 256, 256], P(None, 'chan')
All inputs are finite; a program needn't handle non-finite values.
Results may differ from a plain program's by a relative error of at most 0.0057.
Values may be sent and summed in bfloat16 or wider, within the bound.
No kernel may reach another device: no remote copies, remote signals or barrier semaphores. Data moves between devices by JAX's collectives and lax.ppermute only.
A program may use at most 128 MiB of HBM per device.

v0:
```python
import jax
import jax.numpy as jnp
from jax import lax
from jax.sharding import PartitionSpec as P

GSCALE = 1024
dilations = (6, 12, 18)


def shifted(block, axis, distance):
    devices = range(lax.axis_size(axis))
    route = [(i - distance, i) for i in devices if i - distance in devices]
    if not route:
        return jnp.zeros_like(block)
    return lax.ppermute(block, axis, route)


def from_device(block, ahead):
    return block if ahead == 0 else shifted(block, "band", -ahead)


def rows_at(field, offset):
    height = field.shape[1]
    ahead, start = divmod(offset, height)
    if start == 0:
        return from_device(field, ahead)
    return jnp.concatenate(
        [from_device(field[:, start:], ahead), from_device(field[:, :start], ahead + 1)], axis=1
    )


def local(features, depth_kernel, pointwise, cotangent):
    kernel = depth_kernel.astype(jnp.float32)
    feat_rows = {0: features}
    for spacing in dilations:
        for side in (-1, 1):
            feat_rows[side * spacing] = rows_at(features, side * spacing)
    feat_rows = {k: v.astype(jnp.float32) for k, v in feat_rows.items()}
    branches = [features]
    for which, spacing in enumerate(dilations):
        total = jnp.zeros(features.shape, jnp.float32)
        for tap_index in range(9):
            row_step = tap_index // 3 - 1
            col_step = tap_index % 3 - 1
            total = total + kernel[which, tap_index][:, None, None] * jnp.roll(
                feat_rows[row_step * spacing], -col_step * spacing, axis=-1
            )
        branches.append(total.astype(jnp.bfloat16))
    stacked = jnp.stack(branches)
    output = lax.psum_scatter(
        jnp.einsum("bchw,bco->ohw", stacked, pointwise, preferred_element_type=jnp.float32).astype(
            jnp.bfloat16
        ),
        "chan",
        scatter_dimension=0,
        tiled=True,
    )
    cot_full = lax.all_gather(cotangent, "chan", axis=0, tiled=True)
    grad_sum = jnp.einsum("bco,ohw->bchw", pointwise, cot_full, preferred_element_type=jnp.float32)
    point_local = jnp.einsum("bchw,ohw->bco", stacked, cot_full, preferred_element_type=jnp.float32)
    grad_branches = grad_sum.astype(jnp.bfloat16)
    grad_input = grad_branches[0].astype(jnp.float32)
    depth_rows = []
    for which, spacing in enumerate(dilations):
        grad_field = grad_branches[which + 1]
        grad_f = grad_field.astype(jnp.float32)
        grad_rows = {0: grad_f}
        for side in (-1, 1):
            grad_rows[side * spacing] = rows_at(grad_field, side * spacing).astype(jnp.float32)
        tap_rows = []
        for tap_index in range(9):
            row_step = tap_index // 3 - 1
            col_step = tap_index % 3 - 1
            grad_input = grad_input + kernel[which, tap_index][:, None, None] * jnp.roll(
                grad_rows[-row_step * spacing], col_step * spacing, axis=-1
            )
            tap_rows.append(
                jnp.sum(
                    grad_f * jnp.roll(feat_rows[row_step * spacing], -col_step * spacing, axis=-1),
                    axis=(1, 2),
                )
            )
        depth_rows.append(jnp.stack(tap_rows))
    depth_local = jnp.stack(depth_rows)
    flat = jnp.concatenate([depth_local.reshape(-1), point_local.reshape(-1)])
    flat = lax.psum(flat, "band")
    depth_total = flat[: depth_local.size].reshape(depth_local.shape)
    point_total = flat[depth_local.size :].reshape(point_local.shape)
    return (output, grad_input, depth_total / GSCALE, point_total / GSCALE)


def solution(mesh):
    return jax.shard_map(
        local,
        mesh=mesh,
        in_specs=(
            P("chan", "band", None),
            P(None, None, "chan"),
            P(None, "chan", None),
            P("chan", "band", None),
        ),
        out_specs=(
            P("chan", "band", None),
            P("chan", "band", None),
            P(None, None, "chan"),
            P(None, "chan", None),
        ),
        check_vma=False,
    )
```

profile of v0, /device:TPU:0, one launch (start us, length us, event | category | flops | bytes accessed | tf_op | source)
XLA Modules:
  0.0 347.8 jit_solution(9047192822826043685)
XLA Ops:
  11.5 5.1 %collective-permute-start.6 = (bf16[128,2,1024]{0,2,1:T(8,128)(2,1)}, bf16[128,2,1024]{0,2,1:T(8,128)(2,1)S(1)}, u32[]{:S(2)}, u32[]{:S(2)}) collective-permute-start(bf16[128,2,1024]{0,2,1:T(8,128)(2,1)} %get-tuple-element.125), channel_id=1, source_target_pairs={{0,10},{2,12},{4,14},{6,16},{8,18},{10,20},{12,22},{14,24},{16,26}... | collective-permute-start | bytes 1572872 | tf_op jit(solution)/shard_map/ppermute | solution.py:15
  17.9 7.0 %collective-permute-start = (bf16[128,2,1024]{0,2,1:T(8,128)(2,1)}, bf16[128,2,1024]{0,2,1:T(8,128)(2,1)}, u32[]{:S(2)}, u32[]{:S(2)}) collective-permute-start(bf16[128,2,1024]{0,2,1:T(8,128)(2,1)} %get-tuple-element.125), channel_id=1, source_target_pairs={{0,4},{2,6},{4,8},{6,10},{8,12},{10,14},{12,16},{14,18},{16,20},{1... | collective-permute-start | bytes 1572872 | tf_op jit(solution)/shard_map/ppermute | solution.py:15
  26.3 2.7 collective-permute-start.7
  34.1 7.1 %collective-permute-done.7 = bf16[128,2,1024]{0,2,1:T(8,128)(2,1)S(1)} collective-permute-done((bf16[128,2,1024]{0,2,1:T(8,128)(2,1)}, bf16[128,2,1024]{0,2,1:T(8,128)(2,1)S(1)}, u32[]{:S(2)}, u32[]{:S(2)}) %collective-permute-start.7) | collective-permute-done | bytes 524320 | tf_op jit(solution)/shard_map/ppermute | solution.py:15
  42.7 2.3 fusion.104
  50.4 19.0 %collective-permute-start.4 = (bf16[128,4,1024]{0,2,1:T(8,128)(2,1)S(1)}, bf16[128,4,1024]{0,2,1:T(8,128)(2,1)S(1)}, u32[]{:S(2)}, u32[]{:S(2)}) collective-permute-start(bf16[128,4,1024]{0,2,1:T(8,128)(2,1)S(1)} %copy.35), channel_id=1, source_target_pairs={{0,6},{2,8},{4,10},{6,12},{8,14},{10,16},{12,18},{14,20},{16,22},{... | collective-permute-start | bytes 3145736 | tf_op jit(solution)/shard_map/ppermute | solution.py:15
  74.7 7.1 %fusion.75 = bf16[1,128,4,1024]{1,3,0,2:T(8,128)(2,1)} fusion(f32[128,4,18]{0,2,1:T(8,128)S(1)} %get-tuple-element.90, f32[128,4,1006]{0,2,1:T(8,128)} %get-tuple-element.92, f32[128]{0:T(128)S(1)} %get-tuple-element.128, f32[128]{0:T(128)S(1)} %get-tuple-element.129, f32[128,4,1006]{0,2,1:T(8,128)} %get-tuple-element.91, ...), kind=kLoop, calls=%fused_computation.159 | loop fusion | flops 15204352 | bytes 16781824 | tf_op jit(solution)/shard_map/stack | solution.py:49
  82.0 5.8 %fusion.77 = bf16[1,128,4,1024]{1,3,0,2:T(8,128)(2,1)} fusion(f32[128,4,6]{0,2,1:T(8,128)S(1)} %get-tuple-element.82, f32[128,4,1018]{0,2,1:T(8,128)S(1)} %get-tuple-element.84, f32[128]{0:T(128)} %get-tuple-element.147, f32[128]{0:T(128)} %get-tuple-element.148, f32[128,4,1018]{0,2,1:T(8,128)S(1)} %get-tuple-element.83, ...), kind=kLoop, calls=%fused_computation.161 | loop fusion | flops 15204352 | bytes 16781824 | tf_op jit(solution)/shard_map/stack | solution.py:49
  87.9 9.6 %collective-permute-done.4 = bf16[128,4,1024]{0,2,1:T(8,128)(2,1)S(1)} collective-permute-done((bf16[128,4,1024]{0,2,1:T(8,128)(2,1)S(1)}, bf16[128,4,1024]{0,2,1:T(8,128)(2,1)S(1)}, u32[]{:S(2)}, u32[]{:S(2)}) %collective-permute-start.4) | collective-permute-done | bytes 1048608 | tf_op jit(solution)/shard_map/ppermute | solution.py:15
  101.3 4.3 %fusion.76 = bf16[1,128,4,1024]{1,3,0,2:T(8,128)(2,1)} fusion(f32[128,4,12]{0,2,1:T(8,128)S(1)} %get-tuple-element.118, f32[128,4,1012]{0,2,1:T(8,128)S(1)} %get-tuple-element.120, f32[128]{0:T(128)S(1)} %copy-done.97, bf16[128,4,1024]{0,2,1:T(8,128)(2,1)S(1)} %collective-permute-done.5, f32[128]{0:T(128)S(1)} %copy-done.98, ...), kind=kLoop, calls=%fused_computation.160 | loop fusion | flops 14155776 | bytes 16781824 | tf_op jit(solution)/shard_map/stack | solution.py:49
  105.7 3.0 convolution_convert_fusion
  109.2 5.9 %fusion.47 = (f32[128]{0:T(128)}, f32[128]{0:T(128)}, f32[128]{0:T(128)}, f32[128]{0:T(128)}, f32[128]{0:T(128)}, /*index=5*/f32[128]{0:T(128)}) fusion(f32[128,4,1018]{0,2,1:T(8,128)S(1)} %copy-done.15, f32[128,4,6]{0,2,1:T(8,128)S(1)} %copy-done.84, bf16[4,128,4,1024]{1,3,2,0:T(8,128)(2,1)S(1)} %convolution_convert_fusion, ...), kind=kLoop, calls=%fused_computation.83 | loop fusion | flops 10484992 | bytes 14683136 | tf_op jit(solution)/shard_map/reduce_sum | solution.py:78
  118.5 4.5 %fusion.48 = (f32[128]{0:T(128)}, f32[128]{0:T(128)}, f32[128]{0:T(128)}, f32[128]{0:T(128)}, f32[128]{0:T(128)}, /*index=5*/f32[128]{0:T(128)}, f32[128]{0:T(128)}) fusion(bf16[128,2,1024]{0,2,1:T(8,128)(2,1)S(1)} %copy-done.41, bf16[128,2,1024]{0,2,1:T(8,128)(2,1)} %collective-permute-done.2, bf16[4,128,4,1024]{1,3,2,0:T(8,128)(2,1)S(1)} %convolution_convert_fusion, ...), kind=kLoop, calls=%fused_computation.84 | loop fusion | flops 13630592 | bytes 13635072 | tf_op jit(solution)/shard_map/reduce_sum | solution.py:78
  123.1 4.9 %fusion.45 = (f32[128]{0:T(128)}, f32[128]{0:T(128)}, f32[128]{0:T(128)}, f32[128]{0:T(128)}, f32[128]{0:T(128)}, /*index=5*/f32[128]{0:T(128)}, f32[128]{0:T(128)}, f32[128]{0:T(128)}) fusion(bf16[128,4,1024]{0,2,1:T(8,128)(2,1)S(1)} %copy.35, bf16[4,128,4,1024]{1,3,2,0:T(8,128)(2,1)S(1)} %convolution_convert_fusion, f32[128,4,6]{0,2,1:T(8,128)S(1)} %copy-done.77, ...), kind=kLoop, calls=%fused_computation.81 | loop fusion | flops 13630464 | bytes 13635584 | tf_op jit(solution)/shard_map/reduce_sum | solution.py:78
  128.1 2.5 stack.142
  130.5 6.4 %fusion.49 = (f32[128]{0:T(128)}, f32[128]{0:T(128)}, f32[128]{0:T(128)}, f32[128]{0:T(128)}, f32[128]{0:T(128)}, /*index=5*/f32[128]{0:T(128)}) fusion(f32[128,4,6]{0,2,1:T(8,128)} %copy-done.78, f32[128,4,1018]{0,2,1:T(8,128)S(1)} %copy-done.13, bf16[4,128,4,1024]{1,3,2,0:T(8,128)(2,1)} %copy-done.2, f32[128,4,18]{0,2,1:T(8,128)} %copy-done.57, ...), kind=kLoop, calls=%fused_computation.85 | loop fusion | flops 11009280 | bytes 13634560 | tf_op jit(solution)/shard_map/reduce_sum | solution.py:78
  142.4 3.1 bitcast_convert_fusion
  145.5 3.0 copy.56
  148.5 3.9 %fusion.84 = (f32[128,4,1024]{0,2,1:T(8,128)S(1)}, f32[128,4,1024]{0,2,1:T(8,128)S(1)}, f32[128,4,1024]{0,2,1:T(8,128)S(1)}, bf16[128,4,1024]{0,2,1:T(8,128)(2,1...) fusion(bf16[4,128,4,1024]{1,3,2,0:T(8,128)(2,1)} %copy-done.2), kind=kLoop, calls=%fused_computation.199 | loop fusion | flops 1572864 | bytes 12582912 | tf_op jit(solution)/shard_map/convert_element_type | solution.py:66
  153.5 20.2 %collective-permute-start.18 = (bf16[128,2,1024]{0,2,1:T(8,128)(2,1)}, bf16[128,2,1024]{0,2,1:T(8,128)(2,1)S(1)}, u32[]{:S(2)}, u32[]{:S(2)}) collective-permute-start(bf16[128,2,1024]{0,2,1:T(8,128)(2,1)} %get-tuple-element.93), channel_id=1, source_target_pairs={{0,10},{2,12},{4,14},{6,16},{8,18},{10,20},{12,22},{14,24},{16,26}... | collective-permute-start | bytes 1572872 | tf_op jit(solution)/shard_map/ppermute | solution.py:15
  175.0 5.6 %collective-permute-start.19 = (bf16[128,2,1024]{0,2,1:T(8,128)(2,1)}, bf16[128,2,1024]{0,2,1:T(8,128)(2,1)S(1)}, u32[]{:S(2)}, u32[]{:S(2)}) collective-permute-start(bf16[128,2,1024]{0,2,1:T(8,128)(2,1)} %get-tuple-element.94), channel_id=1, source_target_pairs={{0,8},{2,10},{4,12},{6,14},{8,16},{10,18},{12,20},{14,22},{16,24},... | collective-permute-start | bytes 1572872 | tf_op jit(solution)/shard_map/ppermute | solution.py:15
  184.2 2.4 fusion.92
  186.6 2.4 fusion.96
  190.0 2.9 collective-permute-start.12
  192.9 66.5 %all-reduce.2.cloned.1.call-done = f32[134528]{0:T(1024)} async-done(((f32[134528]{0:T(1024)}), f32[134528]{0:T(1024)}) %all-reduce.2.cloned.1.call-update) | async-done | bytes 538128 | tf_op jit(solution)/shard_map/psum | solution.py:86
  264.1 3.1 collective-permute-start.13
  267.3 2.4 fusion.90
  271.0 6.0 %collective-permute-start.15 = (bf16[128,4,1024]{0,2,1:T(8,128)(2,1)S(1)}, bf16[128,4,1024]{0,2,1:T(8,128)(2,1)S(1)}, u32[]{:S(2)}, u32[]{:S(2)}) collective-permute-start(bf16[128,4,1024]{0,2,1:T(8,128)(2,1)S(1)} %copy-done.54), channel_id=1, source_target_pairs={{0,6},{2,8},{4,10},{6,12},{8,14},{10,16},{12,18},{14,20},{16,22},{... | collective-permute-start | bytes 3145736 | tf_op jit(solution)/shard_map/ppermute | solution.py:15
  280.7 4.8 %collective-permute-done.11 = bf16[128,2,1024]{0,2,1:T(8,128)(2,1)S(1)} collective-permute-done((bf16[128,2,1024]{0,2,1:T(8,128)(2,1)}, bf16[128,2,1024]{0,2,1:T(8,128)(2,1)S(1)}, u32[]{:S(2)}, u32[]{:S(2)}) %collective-permute-start.11) | collective-permute-done | bytes 524320 | tf_op jit(solution)/shard_map/ppermute | solution.py:15
  288.3 24.8 %collective-permute-done.15 = bf16[128,4,1024]{0,2,1:T(8,128)(2,1)S(1)} collective-permute-done((bf16[128,4,1024]{0,2,1:T(8,128)(2,1)S(1)}, bf16[128,4,1024]{0,2,1:T(8,128)(2,1)S(1)}, u32[]{:S(2)}, u32[]{:S(2)}) %collective-permute-start.15) | collective-permute-done | bytes 1048608 | tf_op jit(solution)/shard_map/ppermute | solution.py:15
  315.4 2.4 fusion.109
  320.4 15.6 %fusion.40 = f32[128,4,1024]{0,2,1:T(8,128)S(1)} fusion(f32[128,4,6]{0,2,1:T(8,128)S(1)} %get-tuple-element.74, f32[128,4,1018]{0,2,1:T(8,128)S(1)} %get-tuple-element.76, f32[128,4,1018]{0,2,1:T(8,128)S(1)} %get-tuple-element.75, f32[128,4,6]{0,2,1:T(8,128)S(1)} %get-tuple-element.73, f32[128,4,6]{0,2,1:T(8,128)S(1)} %get-tuple-element.70, ...), kind=kLoop, calls=%fused_computation.76 | loop fusion | flops 45088768 | bytes 50345472 | tf_op jit(solution)/shard_map/add | solution.py:74
  (309 shorter events, 66.2 us)
Async XLA Ops:
  7.2 98.4 %copy-start = (bf16[4,128,256]{2,1,0:T(8,128)(2,1)S(1)}, bf16[4,128,256]{2,1,0:T(8,128)(2,1)}, u32[]{:S(2)}) copy-start(bf16[4,128,256]{2,1,0:T(8,128)(2,1)} %param.6) | copy-start | bytes 786436
  7.2 98.4 %all-gather.2.cloned.1.call-start = ((), (), s32[]{:S(2)}) async-start(), calls=%async_computation.1 | async-start | bytes 3145728 | tf_op jit(solution)/shard_map/all_gather | solution.py:58
  10.2 34.8 %collective-permute-start.8 = (bf16[128,2,1024]{0,2,1:T(8,128)(2,1)}, bf16[128,2,1024]{0,2,1:T(8,128)(2,1)S(1)}, u32[]{:S(2)}, u32[]{:S(2)}) collective-permute-start(bf16[128,2,1024]{0,2,1:T(8,128)(2,1)} %get-tuple-element.125), channel_id=1, source_target_pairs={{8,0},{10,2},{12,4},{14,6},{16,8},{18,10},{20,12},{22,14},{24,16},... | collective-permute-start | bytes 1572872 | tf_op jit(solution)/shard_map/ppermute | solution.py:15
  11.5 21.3 %collective-permute-start.6 = (bf16[128,2,1024]{0,2,1:T(8,128)(2,1)}, bf16[128,2,1024]{0,2,1:T(8,128)(2,1)S(1)}, u32[]{:S(2)}, u32[]{:S(2)}) collective-permute-start(bf16[128,2,1024]{0,2,1:T(8,128)(2,1)} %get-tuple-element.125), channel_id=1, source_target_pairs={{0,10},{2,12},{4,14},{6,16},{8,18},{10,20},{12,22},{14,24},{16,26}... | collective-permute-start | bytes 1572872 | tf_op jit(solution)/shard_map/ppermute | solution.py:15
  16.6 33.8 %collective-permute-start.2 = (bf16[128,2,1024]{0,2,1:T(8,128)(2,1)}, bf16[128,2,1024]{0,2,1:T(8,128)(2,1)}, u32[]{:S(2)}, u32[]{:S(2)}) collective-permute-start(bf16[128,2,1024]{0,2,1:T(8,128)(2,1)} %get-tuple-element.125), channel_id=1, source_target_pairs={{2,0},{4,2},{6,4},{8,6},{10,8},{12,10},{14,12},{16,14},{18,16},{20... | collective-permute-start | bytes 1572872 | tf_op jit(solution)/shard_map/ppermute | solution.py:15
  17.9 53.2 %collective-permute-start = (bf16[128,2,1024]{0,2,1:T(8,128)(2,1)}, bf16[128,2,1024]{0,2,1:T(8,128)(2,1)}, u32[]{:S(2)}, u32[]{:S(2)}) collective-permute-start(bf16[128,2,1024]{0,2,1:T(8,128)(2,1)} %get-tuple-element.125), channel_id=1, source_target_pairs={{0,4},{2,6},{4,8},{6,10},{8,12},{10,14},{12,16},{14,18},{16,20},{1... | collective-permute-start | bytes 1572872 | tf_op jit(solution)/shard_map/ppermute | solution.py:15
  26.3 233.1 %all-reduce.2.cloned.1.call-start = ((), (), s32[]{:S(2)}) async-start(), calls=%async_computation.2 | async-start | bytes 1081344 | tf_op jit(solution)/shard_map/psum | solution.py:86
  26.3 14.9 %collective-permute-start.7 = (bf16[128,2,1024]{0,2,1:T(8,128)(2,1)}, bf16[128,2,1024]{0,2,1:T(8,128)(2,1)S(1)}, u32[]{:S(2)}, u32[]{:S(2)}) collective-permute-start(bf16[128,2,1024]{0,2,1:T(8,128)(2,1)} %get-tuple-element.126), channel_id=1, source_target_pairs={{0,8},{2,10},{4,12},{6,14},{8,16},{10,18},{12,20},{14,22},{16,24},... | collective-permute-start | bytes 1572872 | tf_op jit(solution)/shard_map/ppermute | solution.py:15
  29.0 52.9 %copy-start.74 = (f32[128,4,6]{0,2,1:T(8,128)}, f32[128,4,6]{0,2,1:T(8,128)S(1)}, u32[]{:S(2)}) copy-start(f32[128,4,6]{0,2,1:T(8,128)S(1)} %get-tuple-element.105) | copy-start | bytes 36868
  29.0 52.9 %copy-start.76 = (f32[128,4,6]{0,2,1:T(8,128)}, f32[128,4,6]{0,2,1:T(8,128)S(1)}, u32[]{:S(2)}) copy-start(f32[128,4,6]{0,2,1:T(8,128)S(1)} %get-tuple-element.106) | copy-start | bytes 36868
  29.1 70.9 %copy-start.62 = (f32[128,4,12]{0,2,1:T(8,128)}, f32[128,4,12]{0,2,1:T(8,128)S(1)}, u32[]{:S(2)}) copy-start(f32[128,4,12]{0,2,1:T(8,128)S(1)} %get-tuple-element.113) | copy-start | bytes 73732
  29.1 70.9 %copy-start.64 = (f32[128,4,12]{0,2,1:T(8,128)}, f32[128,4,12]{0,2,1:T(8,128)S(1)}, u32[]{:S(2)}) copy-start(f32[128,4,12]{0,2,1:T(8,128)S(1)} %get-tuple-element.114) | copy-start | bytes 73732
  30.1 69.8 %copy-start.16 = (f32[128,4,1012]{0,2,1:T(8,128)}, f32[128,4,1012]{0,2,1:T(8,128)S(1)}, u32[]{:S(2)}) copy-start(f32[128,4,1012]{0,2,1:T(8,128)S(1)} %get-tuple-element.115) | copy-start | bytes 6217732
  30.1 69.8 %copy-start.18 = (f32[128,4,1012]{0,2,1:T(8,128)}, f32[128,4,1012]{0,2,1:T(8,128)S(1)}, u32[]{:S(2)}) copy-start(f32[128,4,1012]{0,2,1:T(8,128)S(1)} %get-tuple-element.116) | copy-start | bytes 6217732
  31.4 50.5 %copy-start.86 = (f32[128]{0:T(128)}, f32[128]{0:T(128)S(1)}, u32[]{:S(2)}) copy-start(f32[128]{0:T(128)S(1)} %get-tuple-element.127) | copy-start | bytes 1540
  32.8 49.2 %copy-start.4 = (f32[128,4,1018]{0,2,1:T(8,128)}, f32[128,4,1018]{0,2,1:T(8,128)S(1)}, u32[]{:S(2)}) copy-start(f32[128,4,1018]{0,2,1:T(8,128)S(1)} %get-tuple-element.107) | copy-start | bytes 6254596
  32.8 13.9 %collective-permute-start.9 = (bf16[128,2,1024]{0,2,1:T(8,128)(2,1)}, bf16[128,2,1024]{0,2,1:T(8,128)(2,1)S(1)}, u32[]{:S(2)}, u32[]{:S(2)}) collective-permute-start(bf16[128,2,1024]{0,2,1:T(8,128)(2,1)} %get-tuple-element.126), channel_id=1, source_target_pairs={{10,0},{12,2},{14,4},{16,6},{18,8},{20,10},{22,12},{24,14},{26,16}... | collective-permute-start | bytes 1572872 | tf_op jit(solution)/shard_map/ppermute | solution.py:15
  41.2 28.2 %collective-permute-start.3 = (bf16[128,2,1024]{0,2,1:T(8,128)(2,1)}, bf16[128,2,1024]{0,2,1:T(8,128)(2,1)S(1)}, u32[]{:S(2)}, u32[]{:S(2)}) collective-permute-start(bf16[128,2,1024]{0,2,1:T(8,128)(2,1)} %get-tuple-element.126), channel_id=1, source_target_pairs={{4,0},{6,2},{8,4},{10,6},{12,8},{14,10},{16,12},{18,14},{20,16},{2... | collective-permute-start | bytes 1572872 | tf_op jit(solution)/shard_map/ppermute | solution.py:15
  45.0 26.1 %collective-permute-start.1 = (bf16[128,2,1024]{0,2,1:T(8,128)(2,1)}, bf16[128,2,1024]{0,2,1:T(8,128)(2,1)S(1)}, u32[]{:S(2)}, u32[]{:S(2)}) collective-permute-start(bf16[128,2,1024]{0,2,1:T(8,128)(2,1)} %get-tuple-element.126), channel_id=1, source_target_pairs={{0,2},{2,4},{4,6},{6,8},{8,10},{10,12},{12,14},{14,16},{16,18},{18... | collective-permute-start | bytes 1572872 | tf_op jit(solution)/shard_map/ppermute | solution.py:15
  46.7 41.2 %collective-permute-start.5 = (bf16[128,4,1024]{0,2,1:T(8,128)(2,1)S(1)}, bf16[128,4,1024]{0,2,1:T(8,128)(2,1)S(1)}, u32[]{:S(2)}, u32[]{:S(2)}) collective-permute-start(bf16[128,4,1024]{0,2,1:T(8,128)(2,1)S(1)} %copy.35), channel_id=1, source_target_pairs={{6,0},{8,2},{10,4},{12,6},{14,8},{16,10},{18,12},{20,14},{22,16},{... | collective-permute-start | bytes 3145736 | tf_op jit(solution)/shard_map/ppermute | solution.py:15
  50.4 47.1 %collective-permute-start.4 = (bf16[128,4,1024]{0,2,1:T(8,128)(2,1)S(1)}, bf16[128,4,1024]{0,2,1:T(8,128)(2,1)S(1)}, u32[]{:S(2)}, u32[]{:S(2)}) collective-permute-start(bf16[128,4,1024]{0,2,1:T(8,128)(2,1)S(1)} %copy.35), channel_id=1, source_target_pairs={{0,6},{2,8},{4,10},{6,12},{8,14},{10,16},{12,18},{14,20},{16,22},{... | collective-permute-start | bytes 3145736 | tf_op jit(solution)/shard_map/ppermute | solution.py:15
  142.3 195.6 %reduce-scatter.4.cloned.1.call-start = ((), (), s32[]{:S(2)}) async-start(), calls=%async_computation.3 | async-start | bytes 3145728
  153.5 116.2 %collective-permute-start.18 = (bf16[128,2,1024]{0,2,1:T(8,128)(2,1)}, bf16[128,2,1024]{0,2,1:T(8,128)(2,1)S(1)}, u32[]{:S(2)}, u32[]{:S(2)}) collective-permute-start(bf16[128,2,1024]{0,2,1:T(8,128)(2,1)} %get-tuple-element.93), channel_id=1, source_target_pairs={{0,10},{2,12},{4,14},{6,16},{8,18},{10,20},{12,22},{14,24},{16,26}... | collective-permute-start | bytes 1572872 | tf_op jit(solution)/shard_map/ppermute | solution.py:15
  173.7 89.1 %collective-permute-start.16 = (bf16[128,2,1024]{0,2,1:T(8,128)(2,1)}, bf16[128,2,1024]{0,2,1:T(8,128)(2,1)S(1)}, u32[]{:S(2)}, u32[]{:S(2)}) collective-permute-start(bf16[128,2,1024]{0,2,1:T(8,128)(2,1)} %get-tuple-element.93), channel_id=1, source_target_pairs={{8,0},{10,2},{12,4},{14,6},{16,8},{18,10},{20,12},{22,14},{24,16},... | collective-permute-start | bytes 1572872 | tf_op jit(solution)/shard_map/ppermute | solution.py:15
  175.0 96.0 %collective-permute-start.19 = (bf16[128,2,1024]{0,2,1:T(8,128)(2,1)}, bf16[128,2,1024]{0,2,1:T(8,128)(2,1)S(1)}, u32[]{:S(2)}, u32[]{:S(2)}) collective-permute-start(bf16[128,2,1024]{0,2,1:T(8,128)(2,1)} %get-tuple-element.94), channel_id=1, source_target_pairs={{0,8},{2,10},{4,12},{6,14},{8,16},{10,18},{12,20},{14,22},{16,24},... | collective-permute-start | bytes 1572872 | tf_op jit(solution)/shard_map/ppermute | solution.py:15
  180.6 83.5 %collective-permute-start.17 = (bf16[128,2,1024]{0,2,1:T(8,128)(2,1)}, bf16[128,2,1024]{0,2,1:T(8,128)(2,1)S(1)}, u32[]{:S(2)}, u32[]{:S(2)}) collective-permute-start(bf16[128,2,1024]{0,2,1:T(8,128)(2,1)} %get-tuple-element.94), channel_id=1, source_target_pairs={{10,0},{12,2},{14,4},{16,6},{18,8},{20,10},{22,12},{24,14},{26,16}... | collective-permute-start | bytes 1572872 | tf_op jit(solution)/shard_map/ppermute | solution.py:15
  190.0 95.7 %collective-permute-start.12 = (bf16[128,2,1024]{0,2,1:T(8,128)(2,1)}, bf16[128,2,1024]{0,2,1:T(8,128)(2,1)}, u32[]{:S(2)}, u32[]{:S(2)}) collective-permute-start(bf16[128,2,1024]{0,2,1:T(8,128)(2,1)} %get-tuple-element.103), channel_id=1, source_target_pairs={{0,4},{2,6},{4,8},{6,10},{8,12},{10,14},{12,16},{14,18},{16,20},{1... | collective-permute-start | bytes 1572872 | tf_op jit(solution)/shard_map/ppermute | solution.py:15
  262.8 16.6 %collective-permute-start.10 = (bf16[128,2,1024]{0,2,1:T(8,128)(2,1)}, bf16[128,2,1024]{0,2,1:T(8,128)(2,1)S(1)}, u32[]{:S(2)}, u32[]{:S(2)}) collective-permute-start(bf16[128,2,1024]{0,2,1:T(8,128)(2,1)} %get-tuple-element.103), channel_id=1, source_target_pairs={{2,0},{4,2},{6,4},{8,6},{10,8},{12,10},{14,12},{16,14},{18,16},{20... | collective-permute-start | bytes 1572872 | tf_op jit(solution)/shard_map/ppermute | solution.py:15
  264.1 21.6 %collective-permute-start.13 = (bf16[128,2,1024]{0,2,1:T(8,128)(2,1)}, bf16[128,2,1024]{0,2,1:T(8,128)(2,1)S(1)}, u32[]{:S(2)}, u32[]{:S(2)}) collective-permute-start(bf16[128,2,1024]{0,2,1:T(8,128)(2,1)} %get-tuple-element.104), channel_id=1, source_target_pairs={{0,2},{2,4},{4,6},{6,8},{8,10},{10,12},{12,14},{14,16},{16,18},{18... | collective-permute-start | bytes 1572872 | tf_op jit(solution)/shard_map/ppermute | solution.py:15
  269.7 15.8 %collective-permute-start.11 = (bf16[128,2,1024]{0,2,1:T(8,128)(2,1)}, bf16[128,2,1024]{0,2,1:T(8,128)(2,1)S(1)}, u32[]{:S(2)}, u32[]{:S(2)}) collective-permute-start(bf16[128,2,1024]{0,2,1:T(8,128)(2,1)} %get-tuple-element.104), channel_id=1, source_target_pairs={{4,0},{6,2},{8,4},{10,6},{12,8},{14,10},{16,12},{18,14},{20,16},{2... | collective-permute-start | bytes 1572872 | tf_op jit(solution)/shard_map/ppermute | solution.py:15
  271.0 42.1 %collective-permute-start.15 = (bf16[128,4,1024]{0,2,1:T(8,128)(2,1)S(1)}, bf16[128,4,1024]{0,2,1:T(8,128)(2,1)S(1)}, u32[]{:S(2)}, u32[]{:S(2)}) collective-permute-start(bf16[128,4,1024]{0,2,1:T(8,128)(2,1)S(1)} %copy-done.54), channel_id=1, source_target_pairs={{0,6},{2,8},{4,10},{6,12},{8,14},{10,16},{12,18},{14,20},{16,22},{... | collective-permute-start | bytes 3145736 | tf_op jit(solution)/shard_map/ppermute | solution.py:15
  279.4 33.7 %collective-permute-start.14 = (bf16[128,4,1024]{0,2,1:T(8,128)(2,1)S(1)}, bf16[128,4,1024]{0,2,1:T(8,128)(2,1)S(1)}, u32[]{:S(2)}, u32[]{:S(2)}) collective-permute-start(bf16[128,4,1024]{0,2,1:T(8,128)(2,1)S(1)} %copy-done.54), channel_id=1, source_target_pairs={{6,0},{8,2},{10,4},{12,6},{14,8},{16,10},{18,12},{20,14},{22,16},{... | collective-permute-start | bytes 3145736 | tf_op jit(solution)/shard_map/ppermute | solution.py:15
  (97 other events, 1036.1 us)
Sparse Core Ops, SparseCore 0:
  26.4 32.4 all-gather.1
  142.4 116.8 all-reduce.1
  261.6 32.2 reduce-scatter.3
where the time goes:
time: 349 us; the launch traced here: 348 us
  waiting for transfers between devices  113 us (32%)
  starting transfers between devices  86.2 us (25%)
  other arithmetic  67.8 us (19%)
  local copies, waits for them, and re-layouts  58 us (17%)
  between operations  15.4 us (4%)
  matrix products  7.47 us (2%)
    ppermute x20, starting transfers between devices, shifted(): return lax.ppermute(block, axis, route)  86.1 us
    psum x1, waiting for transfers between devices, local(): flat = lax.psum(flat, 'band')  66.5 us
    ppermute x20, waiting for transfers between devices, shifted(): return lax.ppermute(block, axis, route)  46.3 us
    reduce_sum x4, other arithmetic, local(): jnp.sum(grad_f * jnp.roll(feat_rows[row_step * spacing], -col_step * spac...  21.7 us
    unnamed x220, local copies, waits for them, and re-layouts  20.7 us
    slice x18, local copies, waits for them, and re-layouts, local(): jnp.roll(grad_rows[-row_step * spacing], col_step * spacing, axis=-1)  17.5 us
    another operation x3, other arithmetic, local(): stacked = jnp.stack(branches)  17.2 us
    add x1, other arithmetic, local(): grad_input + kernel[which, tap_index][:, None, None] * jnp.roll(grad_rows...  15.6 us
  transfers between devices with their start and end apart: 23, of which 5 were waited for; matrix products, arithmetic and copies ran while one was open for 24% of the time, Pallas kernels for 0%

commit v1 on v0

--- a/solution.py
+++ b/solution.py
@@ -83,7 +83,16 @@
         depth_rows.append(jnp.stack(tap_rows))
     depth_local = jnp.stack(depth_rows)
     flat = jnp.concatenate([depth_local.reshape(-1), point_local.reshape(-1)])
-    flat = lax.psum(flat, "band")
+
+    def numbers_divide(obj):
+        cores_n = lax.axis_size("band")
+        x_next = obj
+        for to_i in [idx for idx in (1, 2, 4, 8, 16) if idx < cores_n]:
+            d_next = lax.ppermute(x_next, "band", [(b, b ^ to_i) for b in range(cores_n)])
+            x_next = x_next + d_next
+        return x_next
+
+    flat = numbers_divide(flat)
     depth_total = flat[: depth_local.size].reshape(depth_local.shape)
     point_total = flat[depth_local.size :].reshape(point_local.shape)
     return (output, grad_input, depth_total / GSCALE, point_total / GSCALE)

time: 349 us -> 304 us (0.87)
  waiting for transfers between devices: 113 us -> 46.2 us
  starting transfers between devices: 86.2 us -> 118 us
  other arithmetic: 67.8 us -> 59.1 us
    psum x1 -> x0, waiting for transfers between devices: 66.5 us -> none  [local(): flat = lax.psum(flat, 'band')]
    ppermute x20, waiting for transfers between devices: 46.3 us -> 17.4 us  [shifted(): return lax.ppermute(block, axis, route)]
    ppermute x0 -> x4, waiting for transfers between devices: none -> 28.7 us  [numbers_divide(): lax.ppermute(x_next, 'band', [(b, b ^ to_i) for b in range(cores_n)])]
    ppermute x0 -> x4, starting transfers between devices: none -> 28.3 us  [numbers_divide(): lax.ppermute(x_next, 'band', [(b, b ^ to_i) for b in range(cores_n)])]
    another operation x3, local copies, waits for them, and re-layouts: 5.21 us -> 0.12 us  [local(): depth_rows.append(jnp.stack(tap_rows))]
    ppermute x20, starting transfers between devices: 86.1 us -> 90.1 us  [shifted(): return lax.ppermute(block, axis, route)]
    unnamed x220 -> x235, local copies, waits for them, and re-layouts: 20.7 us -> 22.5 us
  transfers between devices with their start and end apart: 23 -> 26, of which waited for: 5 -> 5; matrix products, arithmetic and copies ran while one was open for 24% -> 35% of each run, Pallas kernels for 0% -> 0%
where the time goes in v1:
time: 304 us; the launch traced here: 303 us
  starting transfers between devices  118 us (39%)
  other arithmetic  59.1 us (19%)
  local copies, waits for them, and re-layouts  56.4 us (19%)
  waiting for transfers between devices  46.2 us (15%)
  between operations  16 us (5%)
  matrix products  6.76 us (2%)
    ppermute x20, starting transfers between devices, shifted(): return lax.ppermute(block, axis, route)  90.1 us
    ppermute x4, waiting for transfers between devices, numbers_divide(): lax.ppermute(x_next, 'band', [(b, b ^ to_i) for b in range(cores_n)])  28.7 us
    ppermute x4, starting transfers between devices, numbers_divide(): lax.ppermute(x_next, 'band', [(b, b ^ to_i) for b in range(cores_n)])  28.3 us
    unnamed x235, local copies, waits for them, and re-layouts  22.5 us
    slice x18, local copies, waits for them, and re-layouts, local(): jnp.roll(grad_rows[-row_step * spacing], col_step * spacing, axis=-1)  20.6 us
    reduce_sum x4, other arithmetic, local(): jnp.sum(grad_f * jnp.roll(feat_rows[row_step * spacing], -col_step * spac...  19 us
    ppermute x20, waiting for transfers between devices, shifted(): return lax.ppermute(block, axis, route)  17.4 us
    add x1, other arithmetic, local(): grad_input + kernel[which, tap_index][:, None, None] * jnp.roll(grad_rows...  15.9 us
  transfers between devices with their start and end apart: 26, of which 5 were waited for; matrix products, arithmetic and copies ran while one was open for 35% of the time, Pallas kernels for 0%

profile of v1, /device:TPU:0, one launch (start us, length us, event | category | flops | bytes accessed | tf_op | source)
XLA Modules:
  0.0 302.8 jit_solution(15299002375751624634)
XLA Ops:
  11.5 5.1 %collective-permute-start.6 = (bf16[128,2,1024]{0,2,1:T(8,128)(2,1)}, bf16[128,2,1024]{0,2,1:T(8,128)(2,1)S(1)}, u32[]{:S(2)}, u32[]{:S(2)}) collective-permute-start(bf16[128,2,1024]{0,2,1:T(8,128)(2,1)} %get-tuple-element.125), channel_id=1, source_target_pairs={{0,10},{2,12},{4,14},{6,16},{8,18},{10,20},{12,22},{14,24},{16,26}... | collective-permute-start | bytes 1572872 | tf_op jit(solution)/shard_map/ppermute | solution.py:15
  17.9 7.0 %collective-permute-start = (bf16[128,2,1024]{0,2,1:T(8,128)(2,1)}, bf16[128,2,1024]{0,2,1:T(8,128)(2,1)}, u32[]{:S(2)}, u32[]{:S(2)}) collective-permute-start(bf16[128,2,1024]{0,2,1:T(8,128)(2,1)} %get-tuple-element.125), channel_id=1, source_target_pairs={{0,4},{2,6},{4,8},{6,10},{8,12},{10,14},{12,16},{14,18},{16,20},{1... | collective-permute-start | bytes 1572872 | tf_op jit(solution)/shard_map/ppermute | solution.py:15
  26.3 2.7 collective-permute-start.7
  33.9 7.3 %collective-permute-done.7 = bf16[128,2,1024]{0,2,1:T(8,128)(2,1)S(1)} collective-permute-done((bf16[128,2,1024]{0,2,1:T(8,128)(2,1)}, bf16[128,2,1024]{0,2,1:T(8,128)(2,1)S(1)}, u32[]{:S(2)}, u32[]{:S(2)}) %collective-permute-start.7) | collective-permute-done | bytes 524320 | tf_op jit(solution)/shard_map/ppermute | solution.py:15
  50.4 19.1 %collective-permute-start.4 = (bf16[128,4,1024]{0,2,1:T(8,128)(2,1)S(1)}, bf16[128,4,1024]{0,2,1:T(8,128)(2,1)S(1)}, u32[]{:S(2)}, u32[]{:S(2)}) collective-permute-start(bf16[128,4,1024]{0,2,1:T(8,128)(2,1)S(1)} %copy.35), channel_id=1, source_target_pairs={{0,6},{2,8},{4,10},{6,12},{8,14},{10,16},{12,18},{14,20},{16,22},{... | collective-permute-start | bytes 3145736 | tf_op jit(solution)/shard_map/ppermute | solution.py:15
  75.3 6.8 %fusion.75 = bf16[1,128,4,1024]{1,3,0,2:T(8,128)(2,1)} fusion(f32[128,4,18]{0,2,1:T(8,128)S(1)} %get-tuple-element.90, f32[128,4,1006]{0,2,1:T(8,128)} %get-tuple-element.92, f32[128]{0:T(128)S(1)} %get-tuple-element.128, f32[128]{0:T(128)S(1)} %get-tuple-element.129, f32[128,4,1006]{0,2,1:T(8,128)} %get-tuple-element.91, ...), kind=kLoop, calls=%fused_computation.159 | loop fusion | flops 15204352 | bytes 16781824 | tf_op jit(solution)/shard_map/stack | solution.py:49
  82.2 5.0 %fusion.77 = bf16[1,128,4,1024]{1,3,0,2:T(8,128)(2,1)S(1)} fusion(f32[128,4,6]{0,2,1:T(8,128)S(1)} %get-tuple-element.82, f32[128,4,1018]{0,2,1:T(8,128)S(1)} %get-tuple-element.84, f32[128]{0:T(128)} %get-tuple-element.147, f32[128]{0:T(128)} %get-tuple-element.148, f32[128,4,1018]{0,2,1:T(8,128)S(1)} %get-tuple-element.83, ...), kind=kLoop, calls=%fused_computation.161 | loop fusion | flops 15204352 | bytes 16781824 | tf_op jit(solution)/shard_map/stack | solution.py:49
  87.4 10.1 %collective-permute-done.4 = bf16[128,4,1024]{0,2,1:T(8,128)(2,1)S(1)} collective-permute-done((bf16[128,4,1024]{0,2,1:T(8,128)(2,1)S(1)}, bf16[128,4,1024]{0,2,1:T(8,128)(2,1)S(1)}, u32[]{:S(2)}, u32[]{:S(2)}) %collective-permute-start.4) | collective-permute-done | bytes 1048608 | tf_op jit(solution)/shard_map/ppermute | solution.py:15
  102.1 2.4 bitcast_convert_fusion
  104.6 4.1 %copy.56 = bf16[256,4096]{1,0:T(8,128)(2,1)} copy(bf16[256,4096]{0,1:T(8,128)(2,1)} %bitcast.200) | data formatting | bytes 4194304
  108.8 3.0 %convolution_convert_fusion = bf16[4,128,4,1024]{1,3,2,0:T(8,128)(2,1)S(1)} fusion(bf16[256,4,1024]{2,0,1:T(8,128)(2,1)} %all-gather.2.cloned.1.call-done, bf16[4,128,256]{2,1,0:T(8,128)(2,1)S(1)} %copy-done), kind=kOutput, calls=%fused_computation.35 | convolution fusion | flops 1075838976 | bytes 6553600 | tf_op jit(solution)/shard_map/bco,ohw->bchw/dot_general | solution.py:59
  112.3 5.2 %fusion.47 = (f32[128]{0:T(128)S(1)}, f32[128]{0:T(128)S(1)}, f32[128]{0:T(128)S(1)}, f32[128]{0:T(128)S(1)}, f32[128]{0:T(128)S(1)}, /*index=5*/f32[128]{0:T(128)S(1)}) fusion(f32[128,4,1018]{0,2,1:T(8,128)S(1)} %copy-done.16, f32[128,4,6]{0,2,1:T(8,128)S(1)} %copy-done.89, bf16[4,128,4,1024]{1,3,2,0:T(8,128)(2,1)S(1)} %convolution_convert_fusion, ...), kind=kLoop, calls=%fused_computation.83 | loop fusion | flops 10484992 | bytes 14683136 | tf_op jit(solution)/shard_map/reduce_sum | solution.py:78
  117.5 2.7 fusion.84
  121.2 20.4 %collective-permute-start.18 = (bf16[128,2,1024]{0,2,1:T(8,128)(2,1)}, bf16[128,2,1024]{0,2,1:T(8,128)(2,1)}, u32[]{:S(2)}, u32[]{:S(2)}) collective-permute-start(bf16[128,2,1024]{0,2,1:T(8,128)(2,1)} %get-tuple-element.93), channel_id=1, source_target_pairs={{0,10},{2,12},{4,14},{6,16},{8,18},{10,20},{12,22},{14,24},{16,26}... | collective-permute-start | bytes 1572872 | tf_op jit(solution)/shard_map/ppermute | solution.py:15
  142.9 6.3 %collective-permute-start.19 = (bf16[128,2,1024]{0,2,1:T(8,128)(2,1)}, bf16[128,2,1024]{0,2,1:T(8,128)(2,1)}, u32[]{:S(2)}, u32[]{:S(2)}) collective-permute-start(bf16[128,2,1024]{0,2,1:T(8,128)(2,1)} %get-tuple-element.94), channel_id=1, source_target_pairs={{0,8},{2,10},{4,12},{6,14},{8,16},{10,18},{12,20},{14,22},{16,24},... | collective-permute-start | bytes 1572872 | tf_op jit(solution)/shard_map/ppermute | solution.py:15
  151.4 2.3 fusion.92
  154.3 2.4 fusion.96
  159.1 3.9 %fusion.48 = (f32[128]{0:T(128)S(1)}, f32[128]{0:T(128)S(1)}, f32[128]{0:T(128)S(1)}, f32[128]{0:T(128)S(1)}, f32[128]{0:T(128)S(1)}, /*index=5*/f32[128]{0:T(128)S(1)}, f32[128]{0:T(128)S(1)}) fusion(bf16[128,2,1024]{0,2,1:T(8,128)(2,1)S(1)} %copy-done.44, bf16[128,2,1024]{0,2,1:T(8,128)(2,1)} %collective-permute-done.2, ...), kind=kLoop, calls=%fused_computation.84 | loop fusion | flops 13630592 | bytes 13635072 | tf_op jit(solution)/shard_map/reduce_sum | solution.py:78
  163.1 4.1 %fusion.45 = (f32[128]{0:T(128)S(1)}, f32[128]{0:T(128)S(1)}, f32[128]{0:T(128)S(1)}, f32[128]{0:T(128)S(1)}, f32[128]{0:T(128)S(1)}, /*index=5*/f32[128]{0:T(128)S(1)}, f32[128]{0:T(128)S(1)}, f32[128]{0:T(128)S(1)}) fusion(bf16[128,4,1024]{0,2,1:T(8,128)(2,1)S(1)} %copy.35, bf16[4,128,4,1024]{1,3,2,0:T(8,128)(2,1)S(1)} %convolution_convert_fusion, ...), kind=kLoop, calls=%fused_computation.81 | loop fusion | flops 13630464 | bytes 13635584 | tf_op jit(solution)/shard_map/reduce_sum | solution.py:78
  167.3 5.8 %fusion.49 = (f32[128]{0:T(128)S(1)}, f32[128]{0:T(128)S(1)}, f32[128]{0:T(128)S(1)}, f32[128]{0:T(128)S(1)}, f32[128]{0:T(128)S(1)}, /*index=5*/f32[128]{0:T(128)S(1)}) fusion(f32[128,4,6]{0,2,1:T(8,128)S(1)} %copy-done.83, f32[128,4,1018]{0,2,1:T(8,128)S(1)} %copy-done.14, bf16[4,128,4,1024]{1,3,2,0:T(8,128)(2,1)} %copy-done.2, ...), kind=kLoop, calls=%fused_computation.85 | loop fusion | flops 11009280 | bytes 13634560 | tf_op jit(solution)/shard_map/reduce_sum | solution.py:78
  176.0 2.4 fusion.88
  183.1 4.8 %collective-permute-start.13 = (bf16[128,2,1024]{0,2,1:T(8,128)(2,1)S(1)}, bf16[128,2,1024]{0,2,1:T(8,128)(2,1)S(1)}, u32[]{:S(2)}, u32[]{:S(2)}) collective-permute-start(bf16[128,2,1024]{0,2,1:T(8,128)(2,1)S(1)} %get-tuple-element.104), channel_id=1, source_target_pairs={{0,2},{2,4},{4,6},{6,8},{8,10},{10,12},{12,14},{14,16},{16,18},{18... | collective-permute-start | bytes 1572872 | tf_op jit(solution)/shard_map/ppermute | solution.py:15
  190.6 8.2 %collective-permute-start.15 = (bf16[128,4,1024]{0,2,1:T(8,128)(2,1)S(1)}, bf16[128,4,1024]{0,2,1:T(8,128)(2,1)S(1)}, u32[]{:S(2)}, u32[]{:S(2)}) collective-permute-start(bf16[128,4,1024]{0,2,1:T(8,128)(2,1)S(1)} %copy-done.51), channel_id=1, source_target_pairs={{0,6},{2,8},{4,10},{6,12},{8,14},{10,16},{12,18},{14,20},{16,22},{... | collective-permute-start | bytes 3145736 | tf_op jit(solution)/shard_map/ppermute | solution.py:15
  204.0 20.5 %collective-permute-start.20 = (f32[134528]{0:T(1024)S(1)}, f32[134528]{0:T(1024)S(1)}, u32[]{:S(2)}, u32[]{:S(2)}) collective-permute-start(f32[134528]{0:T(1024)S(1)} %constant_dynamic-update-slice_fusion), channel_id=1, source_target_pairs={{0,2},{2,0},{4,6},{6,4},{8,10},{10,8},{12,14},{14,12},{16,18},{18,... | collective-permute-start | bytes 1614344 | tf_op jit(solution)/shard_map/ppermute | solution.py:91
  229.3 2.9 collective-permute-start.21
  232.9 2.3 fusion.111
  235.3 11.3 %collective-permute-done.21 = f32[134528]{0:T(1024)S(1)} collective-permute-done((f32[134528]{0:T(1024)S(1)}, f32[134528]{0:T(1024)S(1)}, u32[]{:S(2)}, u32[]{:S(2)}) %collective-permute-start.21) | collective-permute-done | bytes 538144 | tf_op jit(solution)/shard_map/ppermute | solution.py:91
  246.6 4.7 %collective-permute-start.22 = (f32[134528]{0:T(1024)S(1)}, f32[134528]{0:T(1024)S(1)}, u32[]{:S(2)}, u32[]{:S(2)}) collective-permute-start(f32[134528]{0:T(1024)S(1)} %add.219), channel_id=1, source_target_pairs={{0,8},{2,10},{4,12},{6,14},{8,0},{10,2},{12,4},{14,6},{16,24},{18,... | collective-permute-start | bytes 1614344 | tf_op jit(solution)/shard_map/ppermute | solution.py:91
  252.0 2.4 fusion.109
  254.4 9.3 %collective-permute-done.22 = f32[134528]{0:T(1024)S(1)} collective-permute-done((f32[134528]{0:T(1024)S(1)}, f32[134528]{0:T(1024)S(1)}, u32[]{:S(2)}, u32[]{:S(2)}) %collective-permute-start.22) | collective-permute-done | bytes 538144 | tf_op jit(solution)/shard_map/ppermute | solution.py:91
  263.9 15.9 %fusion.40 = f32[128,4,1024]{0,2,1:T(8,128)S(1)} fusion(f32[128,4,6]{0,2,1:T(8,128)} %get-tuple-element.74, f32[128,4,1018]{0,2,1:T(8,128)S(1)} %get-tuple-element.76, f32[128,4,1018]{0,2,1:T(8,128)S(1)} %get-tuple-element.75, f32[128,4,6]{0,2,1:T(8,128)} %get-tuple-element.73, f32[128,4,6]{0,2,1:T(8,128)S(1)} %copy-done.92, ...), kind=kLoop, calls=%fused_computation.76 | loop fusion | flops 45088768 | bytes 50345472 | tf_op jit(solution)/shard_map/add | solution.py:74
  281.8 8.1 %collective-permute-done.23 = f32[134528]{0:T(1024)} collective-permute-done((f32[134528]{0:T(1024)S(1)}, f32[134528]{0:T(1024)}, u32[]{:S(2)}, u32[]{:S(2)}) %collective-permute-start.23) | collective-permute-done | bytes 538144 | tf_op jit(solution)/shard_map/ppermute | solution.py:91
  (334 shorter events, 68.3 us)
Async XLA Ops:
  7.2 94.9 %copy-start = (bf16[4,128,256]{2,1,0:T(8,128)(2,1)S(1)}, bf16[4,128,256]{2,1,0:T(8,128)(2,1)}, u32[]{:S(2)}) copy-start(bf16[4,128,256]{2,1,0:T(8,128)(2,1)} %param.6) | copy-start | bytes 786436
  7.2 101.5 %all-gather.2.cloned.1.call-start = ((), (), s32[]{:S(2)}) async-start(), calls=%async_computation.1 | async-start | bytes 3145728 | tf_op jit(solution)/shard_map/all_gather | solution.py:58
  10.3 34.6 %collective-permute-start.8 = (bf16[128,2,1024]{0,2,1:T(8,128)(2,1)}, bf16[128,2,1024]{0,2,1:T(8,128)(2,1)S(1)}, u32[]{:S(2)}, u32[]{:S(2)}) collective-permute-start(bf16[128,2,1024]{0,2,1:T(8,128)(2,1)} %get-tuple-element.125), channel_id=1, source_target_pairs={{8,0},{10,2},{12,4},{14,6},{16,8},{18,10},{20,12},{22,14},{24,16},... | collective-permute-start | bytes 1572872 | tf_op jit(solution)/shard_map/ppermute | solution.py:15
  11.5 21.1 %collective-permute-start.6 = (bf16[128,2,1024]{0,2,1:T(8,128)(2,1)}, bf16[128,2,1024]{0,2,1:T(8,128)(2,1)S(1)}, u32[]{:S(2)}, u32[]{:S(2)}) collective-permute-start(bf16[128,2,1024]{0,2,1:T(8,128)(2,1)} %get-tuple-element.125), channel_id=1, source_target_pairs={{0,10},{2,12},{4,14},{6,16},{8,18},{10,20},{12,22},{14,24},{16,26}... | collective-permute-start | bytes 1572872 | tf_op jit(solution)/shard_map/ppermute | solution.py:15
  16.6 33.7 %collective-permute-start.2 = (bf16[128,2,1024]{0,2,1:T(8,128)(2,1)}, bf16[128,2,1024]{0,2,1:T(8,128)(2,1)}, u32[]{:S(2)}, u32[]{:S(2)}) collective-permute-start(bf16[128,2,1024]{0,2,1:T(8,128)(2,1)} %get-tuple-element.125), channel_id=1, source_target_pairs={{2,0},{4,2},{6,4},{8,6},{10,8},{12,10},{14,12},{16,14},{18,16},{20... | collective-permute-start | bytes 1572872 | tf_op jit(solution)/shard_map/ppermute | solution.py:15
  17.9 53.3 %collective-permute-start = (bf16[128,2,1024]{0,2,1:T(8,128)(2,1)}, bf16[128,2,1024]{0,2,1:T(8,128)(2,1)}, u32[]{:S(2)}, u32[]{:S(2)}) collective-permute-start(bf16[128,2,1024]{0,2,1:T(8,128)(2,1)} %get-tuple-element.125), channel_id=1, source_target_pairs={{0,4},{2,6},{4,8},{6,10},{8,12},{10,14},{12,16},{14,18},{16,20},{1... | collective-permute-start | bytes 1572872 | tf_op jit(solution)/shard_map/ppermute | solution.py:15
  26.2 266.4 %reduce-scatter.4.cloned.1.call-start = ((), (), s32[]{:S(2)}) async-start(), calls=%async_computation.2 | async-start | bytes 3145728
  26.3 14.9 %collective-permute-start.7 = (bf16[128,2,1024]{0,2,1:T(8,128)(2,1)}, bf16[128,2,1024]{0,2,1:T(8,128)(2,1)S(1)}, u32[]{:S(2)}, u32[]{:S(2)}) collective-permute-start(bf16[128,2,1024]{0,2,1:T(8,128)(2,1)} %get-tuple-element.126), channel_id=1, source_target_pairs={{0,8},{2,10},{4,12},{6,14},{8,16},{10,18},{12,20},{14,22},{16,24},... | collective-permute-start | bytes 1572872 | tf_op jit(solution)/shard_map/ppermute | solution.py:15
  29.0 53.2 %copy-start.78 = (f32[128,4,6]{0,2,1:T(8,128)}, f32[128,4,6]{0,2,1:T(8,128)S(1)}, u32[]{:S(2)}) copy-start(f32[128,4,6]{0,2,1:T(8,128)S(1)} %get-tuple-element.105) | copy-start | bytes 36868
  29.0 69.2 %copy-start.66 = (f32[128,4,12]{0,2,1:T(8,128)}, f32[128,4,12]{0,2,1:T(8,128)S(1)}, u32[]{:S(2)}) copy-start(f32[128,4,12]{0,2,1:T(8,128)S(1)} %get-tuple-element.113) | copy-start | bytes 73732
  29.0 69.2 %copy-start.68 = (f32[128,4,12]{0,2,1:T(8,128)}, f32[128,4,12]{0,2,1:T(8,128)S(1)}, u32[]{:S(2)}) copy-start(f32[128,4,12]{0,2,1:T(8,128)S(1)} %get-tuple-element.114) | copy-start | bytes 73732
  30.1 68.1 %copy-start.17 = (f32[128,4,1012]{0,2,1:T(8,128)}, f32[128,4,1012]{0,2,1:T(8,128)S(1)}, u32[]{:S(2)}) copy-start(f32[128,4,1012]{0,2,1:T(8,128)S(1)} %get-tuple-element.115) | copy-start | bytes 6217732
  30.1 68.1 %copy-start.19 = (f32[128,4,1012]{0,2,1:T(8,128)}, f32[128,4,1012]{0,2,1:T(8,128)S(1)}, u32[]{:S(2)}) copy-start(f32[128,4,1012]{0,2,1:T(8,128)S(1)} %get-tuple-element.116) | copy-start | bytes 6217732
  32.6 14.0 %collective-permute-start.9 = (bf16[128,2,1024]{0,2,1:T(8,128)(2,1)}, bf16[128,2,1024]{0,2,1:T(8,128)(2,1)S(1)}, u32[]{:S(2)}, u32[]{:S(2)}) collective-permute-start(bf16[128,2,1024]{0,2,1:T(8,128)(2,1)} %get-tuple-element.126), channel_id=1, source_target_pairs={{10,0},{12,2},{14,4},{16,6},{18,8},{20,10},{22,12},{24,14},{26,16}... | collective-permute-start | bytes 1572872 | tf_op jit(solution)/shard_map/ppermute | solution.py:15
  41.2 28.3 %collective-permute-start.3 = (bf16[128,2,1024]{0,2,1:T(8,128)(2,1)}, bf16[128,2,1024]{0,2,1:T(8,128)(2,1)S(1)}, u32[]{:S(2)}, u32[]{:S(2)}) collective-permute-start(bf16[128,2,1024]{0,2,1:T(8,128)(2,1)} %get-tuple-element.126), channel_id=1, source_target_pairs={{4,0},{6,2},{8,4},{10,6},{12,8},{14,10},{16,12},{18,14},{20,16},{2... | collective-permute-start | bytes 1572872 | tf_op jit(solution)/shard_map/ppermute | solution.py:15
  44.9 26.3 %collective-permute-start.1 = (bf16[128,2,1024]{0,2,1:T(8,128)(2,1)}, bf16[128,2,1024]{0,2,1:T(8,128)(2,1)S(1)}, u32[]{:S(2)}, u32[]{:S(2)}) collective-permute-start(bf16[128,2,1024]{0,2,1:T(8,128)(2,1)} %get-tuple-element.126), channel_id=1, source_target_pairs={{0,2},{2,4},{4,6},{6,8},{8,10},{10,12},{12,14},{14,16},{16,18},{18... | collective-permute-start | bytes 1572872 | tf_op jit(solution)/shard_map/ppermute | solution.py:15
  46.6 40.7 %collective-permute-start.5 = (bf16[128,4,1024]{0,2,1:T(8,128)(2,1)S(1)}, bf16[128,4,1024]{0,2,1:T(8,128)(2,1)S(1)}, u32[]{:S(2)}, u32[]{:S(2)}) collective-permute-start(bf16[128,4,1024]{0,2,1:T(8,128)(2,1)S(1)} %copy.35), channel_id=1, source_target_pairs={{6,0},{8,2},{10,4},{12,6},{14,8},{16,10},{18,12},{20,14},{22,16},{... | collective-permute-start | bytes 3145736 | tf_op jit(solution)/shard_map/ppermute | solution.py:15
  50.4 47.1 %collective-permute-start.4 = (bf16[128,4,1024]{0,2,1:T(8,128)(2,1)S(1)}, bf16[128,4,1024]{0,2,1:T(8,128)(2,1)S(1)}, u32[]{:S(2)}, u32[]{:S(2)}) collective-permute-start(bf16[128,4,1024]{0,2,1:T(8,128)(2,1)S(1)} %copy.35), channel_id=1, source_target_pairs={{0,6},{2,8},{4,10},{6,12},{8,14},{10,16},{12,18},{14,20},{16,22},{... | collective-permute-start | bytes 3145736 | tf_op jit(solution)/shard_map/ppermute | solution.py:15
  121.2 68.1 %collective-permute-start.18 = (bf16[128,2,1024]{0,2,1:T(8,128)(2,1)}, bf16[128,2,1024]{0,2,1:T(8,128)(2,1)}, u32[]{:S(2)}, u32[]{:S(2)}) collective-permute-start(bf16[128,2,1024]{0,2,1:T(8,128)(2,1)} %get-tuple-element.93), channel_id=1, source_target_pairs={{0,10},{2,12},{4,14},{6,16},{8,18},{10,20},{12,22},{14,24},{16,26}... | collective-permute-start | bytes 1572872 | tf_op jit(solution)/shard_map/ppermute | solution.py:15
  141.6 40.1 %collective-permute-start.16 = (bf16[128,2,1024]{0,2,1:T(8,128)(2,1)}, bf16[128,2,1024]{0,2,1:T(8,128)(2,1)}, u32[]{:S(2)}, u32[]{:S(2)}) collective-permute-start(bf16[128,2,1024]{0,2,1:T(8,128)(2,1)} %get-tuple-element.93), channel_id=1, source_target_pairs={{8,0},{10,2},{12,4},{14,6},{16,8},{18,10},{20,12},{22,14},{24,16},... | collective-permute-start | bytes 1572872 | tf_op jit(solution)/shard_map/ppermute | solution.py:15
  142.9 47.7 %collective-permute-start.19 = (bf16[128,2,1024]{0,2,1:T(8,128)(2,1)}, bf16[128,2,1024]{0,2,1:T(8,128)(2,1)}, u32[]{:S(2)}, u32[]{:S(2)}) collective-permute-start(bf16[128,2,1024]{0,2,1:T(8,128)(2,1)} %get-tuple-element.94), channel_id=1, source_target_pairs={{0,8},{2,10},{4,12},{6,14},{8,16},{10,18},{12,20},{14,22},{16,24},... | collective-permute-start | bytes 1572872 | tf_op jit(solution)/shard_map/ppermute | solution.py:15
  149.2 33.9 %collective-permute-start.17 = (bf16[128,2,1024]{0,2,1:T(8,128)(2,1)}, bf16[128,2,1024]{0,2,1:T(8,128)(2,1)}, u32[]{:S(2)}, u32[]{:S(2)}) collective-permute-start(bf16[128,2,1024]{0,2,1:T(8,128)(2,1)} %get-tuple-element.94), channel_id=1, source_target_pairs={{10,0},{12,2},{14,4},{16,6},{18,8},{20,10},{22,12},{24,14},{26,16}... | collective-permute-start | bytes 1572872 | tf_op jit(solution)/shard_map/ppermute | solution.py:15
  174.6 27.8 %collective-permute-start.12 = (bf16[128,2,1024]{0,2,1:T(8,128)(2,1)S(1)}, bf16[128,2,1024]{0,2,1:T(8,128)(2,1)S(1)}, u32[]{:S(2)}, u32[]{:S(2)}) collective-permute-start(bf16[128,2,1024]{0,2,1:T(8,128)(2,1)S(1)} %get-tuple-element.103), channel_id=1, source_target_pairs={{0,4},{2,6},{4,8},{6,10},{8,12},{10,14},{12,16},{14,18},{16,20},{1... | collective-permute-start | bytes 1572872 | tf_op jit(solution)/shard_map/ppermute | solution.py:15
  181.7 45.7 %collective-permute-start.10 = (bf16[128,2,1024]{0,2,1:T(8,128)(2,1)S(1)}, bf16[128,2,1024]{0,2,1:T(8,128)(2,1)S(1)}, u32[]{:S(2)}, u32[]{:S(2)}) collective-permute-start(bf16[128,2,1024]{0,2,1:T(8,128)(2,1)S(1)} %get-tuple-element.103), channel_id=1, source_target_pairs={{2,0},{4,2},{6,4},{8,6},{10,8},{12,10},{14,12},{16,14},{18,16},{20... | collective-permute-start | bytes 1572872 | tf_op jit(solution)/shard_map/ppermute | solution.py:15
  183.1 20.8 %collective-permute-start.13 = (bf16[128,2,1024]{0,2,1:T(8,128)(2,1)S(1)}, bf16[128,2,1024]{0,2,1:T(8,128)(2,1)S(1)}, u32[]{:S(2)}, u32[]{:S(2)}) collective-permute-start(bf16[128,2,1024]{0,2,1:T(8,128)(2,1)S(1)} %get-tuple-element.104), channel_id=1, source_target_pairs={{0,2},{2,4},{4,6},{6,8},{8,10},{10,12},{12,14},{14,16},{16,18},{18... | collective-permute-start | bytes 1572872 | tf_op jit(solution)/shard_map/ppermute | solution.py:15
  189.3 38.1 %collective-permute-start.11 = (bf16[128,2,1024]{0,2,1:T(8,128)(2,1)S(1)}, bf16[128,2,1024]{0,2,1:T(8,128)(2,1)S(1)}, u32[]{:S(2)}, u32[]{:S(2)}) collective-permute-start(bf16[128,2,1024]{0,2,1:T(8,128)(2,1)S(1)} %get-tuple-element.104), channel_id=1, source_target_pairs={{4,0},{6,2},{8,4},{10,6},{12,8},{14,10},{16,12},{18,14},{20,16},{2... | collective-permute-start | bytes 1572872 | tf_op jit(solution)/shard_map/ppermute | solution.py:15
  190.6 60.7 %collective-permute-start.15 = (bf16[128,4,1024]{0,2,1:T(8,128)(2,1)S(1)}, bf16[128,4,1024]{0,2,1:T(8,128)(2,1)S(1)}, u32[]{:S(2)}, u32[]{:S(2)}) collective-permute-start(bf16[128,4,1024]{0,2,1:T(8,128)(2,1)S(1)} %copy-done.51), channel_id=1, source_target_pairs={{0,6},{2,8},{4,10},{6,12},{8,14},{10,16},{12,18},{14,20},{16,22},{... | collective-permute-start | bytes 3145736 | tf_op jit(solution)/shard_map/ppermute | solution.py:15
  202.4 29.9 %collective-permute-start.14 = (bf16[128,4,1024]{0,2,1:T(8,128)(2,1)S(1)}, bf16[128,4,1024]{0,2,1:T(8,128)(2,1)S(1)}, u32[]{:S(2)}, u32[]{:S(2)}) collective-permute-start(bf16[128,4,1024]{0,2,1:T(8,128)(2,1)S(1)} %copy-done.51), channel_id=1, source_target_pairs={{6,0},{8,2},{10,4},{12,6},{14,8},{16,10},{18,12},{20,14},{22,16},{... | collective-permute-start | bytes 3145736 | tf_op jit(solution)/shard_map/ppermute | solution.py:15
  204.0 25.3 %collective-permute-start.20 = (f32[134528]{0:T(1024)S(1)}, f32[134528]{0:T(1024)S(1)}, u32[]{:S(2)}, u32[]{:S(2)}) collective-permute-start(f32[134528]{0:T(1024)S(1)} %constant_dynamic-update-slice_fusion), channel_id=1, source_target_pairs={{0,2},{2,0},{4,6},{6,4},{8,10},{10,8},{12,14},{14,12},{16,18},{18,... | collective-permute-start | bytes 1614344 | tf_op jit(solution)/shard_map/ppermute | solution.py:91
  229.3 17.2 %collective-permute-start.21 = (f32[134528]{0:T(1024)S(1)}, f32[134528]{0:T(1024)S(1)}, u32[]{:S(2)}, u32[]{:S(2)}) collective-permute-start(f32[134528]{0:T(1024)S(1)} %add.218), channel_id=1, source_target_pairs={{0,4},{2,6},{4,0},{6,2},{8,12},{10,14},{12,8},{14,10},{16,20},{18,... | collective-permute-start | bytes 1614344 | tf_op jit(solution)/shard_map/ppermute | solution.py:91
  246.6 17.1 %collective-permute-start.22 = (f32[134528]{0:T(1024)S(1)}, f32[134528]{0:T(1024)S(1)}, u32[]{:S(2)}, u32[]{:S(2)}) collective-permute-start(f32[134528]{0:T(1024)S(1)} %add.219), channel_id=1, source_target_pairs={{0,8},{2,10},{4,12},{6,14},{8,0},{10,2},{12,4},{14,6},{16,24},{18,... | collective-permute-start | bytes 1614344 | tf_op jit(solution)/shard_map/ppermute | solution.py:91
  263.7 26.2 %collective-permute-start.23 = (f32[134528]{0:T(1024)S(1)}, f32[134528]{0:T(1024)}, u32[]{:S(2)}, u32[]{:S(2)}) collective-permute-start(f32[134528]{0:T(1024)S(1)} %add.220), channel_id=1, source_target_pairs={{0,16},{2,18},{4,20},{6,22},{8,24},{10,26},{12,28},{14,30},{16,0},... | collective-permute-start | bytes 1614344 | tf_op jit(solution)/shard_map/ppermute | solution.py:91
  (107 other events, 1277.6 us)
Sparse Core Ops, SparseCore 0:
  26.3 32.4 all-gather.1
  108.8 51.2 reduce-scatter.3
